TPU v7x, 512 devices: a whole 4x8x8 slice. The times are simulated.
512 devices in a mesh: grp: 16 (over x, z_lo), ep: 32 (over y, z_hi, core).
Axes of the slice: x: 4, y: 8, z: 8 (z_hi: 2, z_lo: 4; z = z_hi * 4 + z_lo), core: 2. Of those that a mesh axis runs over, the one named last changes fastest.
Arguments:
- slot_hidden: bfloat16 [65536, 8, 768], P(('grp', 'ep')), may hold values from -6 to 6
- expert_ids: int32 [65536, 8], P(('grp', 'ep')), may hold values from 0 to 63, all different within a row; in each aligned block of 128 rows (0 to 127, 128 to 255, ...) at most 24 rows name the same one
- gate_fixed: int32 [65536, 8], P(('grp', 'ep')), may hold values from 1 to 65535
- master: float32 [64, 768, 2048], P('ep', 'grp'), may hold values from -6 to 6
- moment_one: bfloat16 [64, 768, 2048], P('ep', 'grp'), may hold values from -3 to 3
- moment_two: bfloat16 [64, 768, 2048], P('ep', 'grp'), may hold values from 0.0099487305 to 2
- gradient: bfloat16 [64, 768, 2048], P('ep', 'grp'), may hold values from -6 to 6
Outputs:
- mixed: bfloat16 [65536, 2048], P(('grp', 'ep'))
- backup: float32 [64, 768, 2048], P('ep', 'grp')
Inputs may be any that keep to these rules, and one draw needn't show every extreme that they name: `expert_ids`: in each aligned block of 128 rows (the rows of one device) no expert is named by more than 24 rows, a bound that some block reaches; the 8 experts of a row differ.
All inputs are finite; a program needn't handle non-finite values.
Results may differ from a plain program's by a relative error of at most 0.0057.
Values may be sent and summed in bfloat16 or wider, within the bound.
No kernel may reach another device: no remote copies, remote signals or barrier semaphores. Data moves between devices by JAX's collectives and lax.ppermute only.
A program may use at most 64 MiB of HBM per device.

v0:
```python
import math
import jax
import jax.numpy as jnp
from jax import lax
from jax.sharding import Mesh
from jax.sharding import PartitionSpec as P

GRP = ("grp_0", "grp_1")
beta_one = 0.9
beta_two = 0.95
corr_one = 1.0 - 0.9**40
corr_two = 1.0 - 0.95**40
learn_rate = 0.05
decay_rate = 0.1
adam_eps = 1e-08
gate_unit = 65536.0


def adamw_step(master, moment_one, moment_two, gradient):
    widened = gradient.astype(jnp.float32)
    first_moment = beta_one * moment_one.astype(jnp.float32) + (1.0 - beta_one) * widened
    second_moment = beta_two * moment_two.astype(jnp.float32) + (1.0 - beta_two) * widened * widened
    return (
        first_moment / corr_one / (jnp.sqrt(second_moment / corr_two) + adam_eps)
        + decay_rate * master
    )


def slot_positions(ids, capacity):
    count = ids.shape[0]
    rows = lax.broadcasted_iota(jnp.int32, (count, count), 0)
    cols = lax.broadcasted_iota(jnp.int32, (count, count), 1)
    same = (ids[:, None] == ids[None, :]) & (cols < rows)
    slot_index = jnp.sum(same.astype(jnp.int32), axis=1)
    return ids * capacity + slot_index


def body(slot_hidden, expert_ids, gate_fixed, master, moment_one, moment_two, gradient):
    outer = lax.axis_size("grp_0")
    ranks = lax.axis_size("ep")
    local_experts = master.shape[0]
    experts = local_experts * ranks
    tok_count, top_count, hidden_width = slot_hidden.shape
    width = master.shape[2]
    capacity = max(2, tok_count * top_count // experts + tok_count * top_count // (2 * experts))
    slots = experts * capacity
    scaling = 1.0 / math.sqrt(hidden_width)
    step_dir = adamw_step(master, moment_one, moment_two, gradient)
    updated = master - learn_rate * step_dir
    weights = updated.astype(jnp.bfloat16)
    shift = outer // 2
    backup = lax.ppermute(step_dir, "grp_0", [(s, (s + shift) % outer) for s in range(outer)])
    pairs = tok_count * top_count
    positions = slot_positions(expert_ids.reshape(pairs), capacity)
    hidden_rows = slot_hidden.reshape(pairs, hidden_width)
    token_pos = positions.reshape(tok_count, top_count)
    high = (gate_fixed // 256).astype(jnp.float32) / 256.0
    low = (gate_fixed % 256).astype(jnp.float32) / gate_unit
    chunk = ranks * capacity
    column = lax.broadcasted_iota(jnp.int32, (chunk,), 0)
    slot_of = []
    arrived = []
    for local in range(local_experts):
        slot_of.append((column // capacity * local_experts + local) * capacity + column % capacity)
        placing = (positions[None, :] == slot_of[local][:, None]).astype(jnp.bfloat16)
        outgoing = jnp.dot(placing, hidden_rows, preferred_element_type=jnp.float32).astype(
            jnp.bfloat16
        )
        arrived.append(
            lax.all_to_all(
                outgoing.reshape(ranks, capacity, hidden_width),
                "ep",
                split_axis=0,
                concat_axis=0,
                tiled=True,
            )
        )
    gathered = []
    first_stage = []
    for local in range(local_experts):
        own = weights[local]
        if first_stage:
            own, _ = lax.optimization_barrier((own, arrived[0]))
        rows = lax.all_gather(own, "grp_1", axis=0, tiled=True)
        first_stage.append(rows)
        rows, tie = lax.optimization_barrier((rows, gathered[-1] if gathered else arrived[0]))
        if not gathered:
            arrived[0] = tie
        gathered.append(lax.all_gather(rows, "grp_0", axis=0, tiled=True))
    mixed = jnp.zeros((tok_count, width), jnp.float32)
    for local in range(local_experts):
        product = jnp.dot(
            arrived[local].reshape(chunk, hidden_width),
            gathered[local],
            preferred_element_type=jnp.float32,
        )
        results = (product * scaling).astype(jnp.bfloat16)
        if local + 1 < local_experts:
            results, _ = lax.optimization_barrier((results, first_stage[local + 1]))
        returned = lax.all_to_all(
            results.reshape(ranks, capacity, width), "ep", split_axis=0, concat_axis=0, tiled=True
        )
        returned = returned.reshape(chunk, width)
        hit = token_pos[:, :, None] == slot_of[local][None, None, :]
        weight = jnp.concatenate(
            [jnp.sum(jnp.where(hit, part[:, :, None], 0.0), axis=1) for part in (high, low)], axis=0
        )
        both = jnp.dot(weight.astype(jnp.bfloat16), returned, preferred_element_type=jnp.float32)
        mixed = mixed + both[:tok_count] + both[tok_count:]
    return (mixed.astype(jnp.bfloat16), backup)


def solution(mesh):
    torus = Mesh(mesh.devices.reshape(4, 4, mesh.shape["ep"]), ("grp_0", "grp_1", "ep"))
    tokens = P(GRP + ("ep",), None, None)
    pair_spec = P(GRP + ("ep",), None)
    state = P("ep", GRP, None)
    in_specs = (tokens, pair_spec, pair_spec, state, state, state, state)
    out_specs = (pair_spec, state)
    return jax.shard_map(body, mesh=torus, in_specs=in_specs, out_specs=out_specs, check_vma=False)
```

profile of v0, /device:TPU:188, one launch (start us, length us, event | category | flops | bytes accessed | tf_op | source)
XLA Modules:
  0.0 326.0 jit_solution(854978757086746772)
XLA Ops:
  7.2 0.9 copy.22
  8.1 0.1 eq.33
  8.2 0.5 convert_reduce_fusion
  8.7 2.5 fusion.15
  11.2 13.7 %all-to-all-start = ((bf16[32,24,768]{2,1,0:T(8,128)(2,1)}), bf16[32,24,768]{2,1,0:T(8,128)(2,1)S(1)}, u32[]{:S(2)}, u32[]{:S(2)}) async-start(bf16[32,24,768]{2,1,0:T(8,128)(2,1)} %bitcast.31), calls=%async_computation | async-start | bytes 2359296 | tf_op jit(solution)/shard_map/all_to_all | solution.py:70
  25.0 0.0 all-gather.4.cloned.1.call-start
  25.0 2.8 subtract_convert_fusion
  27.9 39.6 %all-gather = bf16[1,192,2048]{2,1,0:T(8,128)(2,1)} all-gather(bf16[1,48,2048]{2,1,0:T(8,128)(2,1)S(1)} %get-tuple-element.20), channel_id=2, replica_groups=mesh['grp_0'=4,'grp_1'=4,'ep'=32] {'grp_1'}, dimensions={1}, use_global_device_ids=true | all-gather | bytes 983040 | tf_op jit(solution)/shard_map/all_gather | solution.py:84
  67.4 0.0 all-gather.4.cloned.1.call-update
  67.5 2.5 fusion.20
  70.0 10.2 %all-to-all-start.2 = ((bf16[32,24,768]{2,1,0:T(8,128)(2,1)}), bf16[32,24,768]{2,1,0:T(8,128)(2,1)}, u32[]{:S(2)}, u32[]{:S(2)}) async-start(bf16[32,24,768]{2,1,0:T(8,128)(2,1)} %bitcast.30), calls=%async_computation.2 | async-start | bytes 2359296 | tf_op jit(solution)/shard_map/all_to_all | solution.py:70
  80.1 43.1 %all_gather.14 = bf16[192,2048]{1,0:T(8,128)(2,1)} all-gather(bf16[48,2048]{1,0:T(8,128)(2,1)S(1)} %get-tuple-element.9), channel_id=1, replica_groups=mesh['grp_0'=4,'grp_1'=4,'ep'=32] {'grp_1'}, dimensions={0}, use_global_device_ids=true | all-gather | bytes 983040 | tf_op jit(solution)/shard_map/all_gather | solution.py:84
  123.2 5.9 %multiply_convert_fusion.1 = bf16[768,2048]{1,0:T(8,128)(2,1)} fusion(bf16[768,768]{1,0:T(8,128)(2,1)S(1)} %bitcast.29, bf16[768,2048]{1,0:T(8,128)(2,1)} %all-gather.4.cloned.1.call-done), kind=kOutput, calls=%fused_computation.1 | convolution fusion | flops 2419064832 | bytes 7471104 | tf_op jit(solution)/shard_map/dot_general | solution.py:92
  129.2 9.0 %all-to-all-start.1 = ((bf16[32,24,2048]{2,1,0:T(8,128)(2,1)}), bf16[32,24,2048]{2,1,0:T(8,128)(2,1)}, u32[]{:S(2)}, u32[]{:S(2)}) async-start(bf16[32,24,2048]{2,1,0:T(8,128)(2,1)} %bitcast.27), calls=%async_computation.1 | async-start | bytes 6291456 | tf_op jit(solution)/shard_map/all_to_all | solution.py:100
  138.2 0.0 all-gather.6.cloned.1.call-start
  138.3 0.7 all-gather.6.cloned.1.call-update
  139.0 48.5 %all-gather.6.cloned.1.call-done = bf16[768,2048]{1,0:T(8,128)(2,1)} async-done(((bf16[192,2048]{1,0:T(8,128)(2,1)}), bf16[768,2048]{1,0:T(8,128)(2,1)}) %all-gather.6.cloned.1.call-update) | async-done | bytes 3145744 | tf_op jit(solution)/shard_map/all_gather | solution.py:89
  187.5 6.5 %multiply_convert_fusion = bf16[768,2048]{1,0:T(8,128)(2,1)} fusion(bf16[768,768]{1,0:T(8,128)(2,1)} %bitcast.8, bf16[768,2048]{1,0:T(8,128)(2,1)} %all-gather.6.cloned.1.call-done), kind=kOutput, calls=%fused_computation | convolution fusion | flops 2419064832 | bytes 7471104 | tf_op jit(solution)/shard_map/dot_general | solution.py:92
  194.0 27.2 %all-to-all-done.1 = bf16[32,24,2048]{2,1,0:T(8,128)(2,1)} async-done(((bf16[32,24,2048]{2,1,0:T(8,128)(2,1)}), bf16[32,24,2048]{2,1,0:T(8,128)(2,1)}, u32[]{:S(2)}, u32[]{:S(2)}) %all-to-all-start.1) | async-done | bytes 3145760 | tf_op jit(solution)/shard_map/all_to_all | solution.py:100
  221.3 9.3 %all-to-all-start.3 = ((bf16[32,24,2048]{2,1,0:T(8,128)(2,1)}), bf16[32,24,2048]{2,1,0:T(8,128)(2,1)}, u32[]{:S(2)}, u32[]{:S(2)}) async-start(bf16[32,24,2048]{2,1,0:T(8,128)(2,1)} %bitcast.26), calls=%async_computation.3 | async-start | bytes 6291456 | tf_op jit(solution)/shard_map/all_to_all | solution.py:100
  230.6 2.6 collective-permute-start
  233.2 0.1 reduce_sum.48
  233.4 0.8 copy.24
  234.1 0.7 copy.25
  234.8 0.7 copy.26
  235.6 4.6 %fusion.2 = (bf16[128,768]{1,0:T(8,128)(2,1)S(1)}, bf16[128,768]{1,0:T(8,128)(2,1)S(1)}, bf16[128,768]{1,0:T(8,128)(2,1)S(1)}, bf16[128,768]{1,0:T(8,128)(2,1)S(1)}) fusion(f32[128,8]{1,0:T(8,128)} %copy.26, s32[768]{0:T(1024)S(1)} %get-tuple-element.25, s32[128,8]{1,0:T(8,128)} %copy.24, s32[768]{0:T(1024)S(1)} %get-tuple-element.24, f32[128,8]{1,0:T(8,128)} %copy.25), kind=kLoop, calls=%fused_computation.10 | loop fusion | flops 7471104 | bytes 804864 | tf_op jit(solution)/shard_map/reduce_sum | solution.py:106
  240.2 13.4 %collective-permute-done = f32[2,48,2048]{2,1,0:T(8,128)S(1)} collective-permute-done((f32[2,48,2048]{2,1,0:T(8,128)S(1)}, f32[2,48,2048]{2,1,0:T(8,128)S(1)}, u32[]{:S(2)}, u32[]{:S(2)}) %collective-permute-start) | collective-permute-done | bytes 786464 | tf_op jit(solution)/shard_map/ppermute | solution.py:52
  253.6 4.2 %fusion.34 = f32[256,2048]{1,0:T(8,128)} fusion(bf16[768,2048]{1,0:T(8,128)(2,1)} %bitcast.6, bf16[128,768]{1,0:T(8,128)(2,1)S(1)} %get-tuple-element.14, bf16[128,768]{1,0:T(8,128)(2,1)S(1)} %get-tuple-element.17), kind=kOutput, calls=%fused_computation.40 | convolution fusion | flops 806092800 | bytes 5636096 | tf_op jit(solution)/shard_map/dot_general | solution.py:108
  257.8 56.4 %all-to-all-done.3 = bf16[32,24,2048]{2,1,0:T(8,128)(2,1)} async-done(((bf16[32,24,2048]{2,1,0:T(8,128)(2,1)}), bf16[32,24,2048]{2,1,0:T(8,128)(2,1)}, u32[]{:S(2)}, u32[]{:S(2)}) %all-to-all-start.3) | async-done | bytes 3145760 | tf_op jit(solution)/shard_map/all_to_all | solution.py:100
  314.2 3.0 fusion.38
  317.3 1.0 fusion.25
  318.3 0.9 copy.28
  (21 shorter events, 0.1 us)
Async XLA Ops:
  7.2 1.6 copy-start
  8.7 16.3 %copy-start.2 = (f32[2,48,2048]{2,1,0:T(8,128)S(1)}, f32[2,48,2048]{2,1,0:T(8,128)}, u32[]{:S(2)}) copy-start(f32[2,48,2048]{2,1,0:T(8,128)} %param.10) | copy-start | bytes 2359300
  11.2 56.2 %all-to-all-start = ((bf16[32,24,768]{2,1,0:T(8,128)(2,1)}), bf16[32,24,768]{2,1,0:T(8,128)(2,1)S(1)}, u32[]{:S(2)}, u32[]{:S(2)}) async-start(bf16[32,24,768]{2,1,0:T(8,128)(2,1)} %bitcast.31), calls=%async_computation | async-start | bytes 2359296 | tf_op jit(solution)/shard_map/all_to_all | solution.py:70
  25.0 98.3 %all-gather.4.cloned.1.call-start = ((), (), s32[]{:S(2)}) async-start(), calls=%async_computation.4 | async-start | bytes 3932160 | tf_op jit(solution)/shard_map/all_gather | solution.py:89
  70.0 59.2 %all-to-all-start.2 = ((bf16[32,24,768]{2,1,0:T(8,128)(2,1)}), bf16[32,24,768]{2,1,0:T(8,128)(2,1)}, u32[]{:S(2)}, u32[]{:S(2)}) async-start(bf16[32,24,768]{2,1,0:T(8,128)(2,1)} %bitcast.30), calls=%async_computation.2 | async-start | bytes 2359296 | tf_op jit(solution)/shard_map/all_to_all | solution.py:70
  129.2 92.1 %all-to-all-start.1 = ((bf16[32,24,2048]{2,1,0:T(8,128)(2,1)}), bf16[32,24,2048]{2,1,0:T(8,128)(2,1)}, u32[]{:S(2)}, u32[]{:S(2)}) async-start(bf16[32,24,2048]{2,1,0:T(8,128)(2,1)} %bitcast.27), calls=%async_computation.1 | async-start | bytes 6291456 | tf_op jit(solution)/shard_map/all_to_all | solution.py:100
  138.2 49.3 %all-gather.6.cloned.1.call-start = ((), (), s32[]{:S(2)}) async-start(), calls=%async_computation.5 | async-start | bytes 3932160 | tf_op jit(solution)/shard_map/all_gather | solution.py:89
  221.3 9.3 %copy-start.3 = (f32[2,48,2048]{2,1,0:T(8,128)S(1)}, f32[2,48,2048]{2,1,0:T(8,128)}, u32[]{:S(2)}) copy-start(f32[2,48,2048]{2,1,0:T(8,128)} %get-tuple-element.19) | copy-start | bytes 2359300
  221.3 12.1 %copy-start.4 = (s32[128,8]{0,1:T(8,128)S(1)}, s32[128,8]{0,1:T(8,128)}, u32[]{:S(2)}) copy-start(s32[128,8]{0,1:T(8,128)} %param.8) | copy-start | bytes 12292
  221.3 12.9 %copy-start.5 = (s32[128,8]{0,1:T(8,128)S(1)}, s32[128,8]{0,1:T(8,128)}, u32[]{:S(2)}) copy-start(s32[128,8]{0,1:T(8,128)} %param.9) | copy-start | bytes 12292
  221.3 93.0 %all-to-all-start.3 = ((bf16[32,24,2048]{2,1,0:T(8,128)(2,1)}), bf16[32,24,2048]{2,1,0:T(8,128)(2,1)}, u32[]{:S(2)}, u32[]{:S(2)}) async-start(bf16[32,24,2048]{2,1,0:T(8,128)(2,1)} %bitcast.26), calls=%async_computation.3 | async-start | bytes 6291456 | tf_op jit(solution)/shard_map/all_to_all | solution.py:100
  230.6 23.0 %collective-permute-start = (f32[2,48,2048]{2,1,0:T(8,128)S(1)}, f32[2,48,2048]{2,1,0:T(8,128)S(1)}, u32[]{:S(2)}, u32[]{:S(2)}) collective-permute-start(f32[2,48,2048]{2,1,0:T(8,128)S(1)} %copy-done.3), channel_id=1, source_target_pairs={{0,256},{128,384},{256,0},{384,128},{1,257},{129,385},{257,1},{385... | collective-permute-start | bytes 2359304 | tf_op jit(solution)/shard_map/ppermute | solution.py:52
  314.2 3.0 copy-start.1
Sparse Core Ops, SparseCore 0:
  67.6 44.2 all-gather.3
  141.1 46.2 all-gather.5
where the time goes:
time: 327 us; the launch traced here: 326 us
  waiting for transfers between devices  146 us (45%)
  blocking collectives  82.7 us (25%)
  starting transfers between devices  45 us (14%)
  matrix products  24.7 us (8%)
  between operations  14.2 us (4%)
  other arithmetic  9.01 us (3%)
  local copies, waits for them, and re-layouts  4.26 us (1%)
    all_to_all x2, waiting for transfers between devices, body(): lax.all_to_all(results.reshape(ranks, capacity, width), 'ep', split_axis=...  83.7 us
    all_gather x2, blocking collectives, body(): rows = lax.all_gather(own, 'grp_1', axis=0, tiled=True)  82.7 us
    all_gather x2, waiting for transfers between devices, body(): gathered.append(lax.all_gather(rows, 'grp_0', axis=0, tiled=True))  48.5 us
    all_to_all x2, starting transfers between devices, body(): lax.all_to_all(outgoing.reshape(ranks, capacity, hidden_width), 'ep', spl...  23.9 us
    all_to_all x2, starting transfers between devices, body(): lax.all_to_all(results.reshape(ranks, capacity, width), 'ep', split_axis=...  18.3 us
    ppermute x1, waiting for transfers between devices, body(): lax.ppermute(step_dir, 'grp_0', [(s, (s + shift) % outer) for s in range(...  13.4 us
    dot_general x2, matrix products, body(): jnp.dot(arrived[local].reshape(chunk, hidden_width), gathered[local], pre...  12.5 us
    dot_general x2, matrix products, body(): jnp.dot(weight.astype(jnp.bfloat16), returned, preferred_element_type=jnp...  7.24 us
  transfers between devices with their start and end apart: 7, of which 4 were waited for; matrix products, arithmetic and copies ran while one was open for 9% of the time, Pallas kernels for 0%

commit v1 on v0

--- a/solution.py
+++ b/solution.py
@@ -86,7 +86,11 @@
         rows, tie = lax.optimization_barrier((rows, gathered[-1] if gathered else arrived[0]))
         if not gathered:
             arrived[0] = tie
-        gathered.append(lax.all_gather(rows, "grp_0", axis=0, tiled=True))
+        gathered.append(
+            jnp.concatenate(
+                lax.all_to_all(jnp.stack([rows] * lax.axis_size("grp_0")), "grp_0", 0, 0), axis=0
+            )
+        )
     mixed = jnp.zeros((tok_count, width), jnp.float32)
     for local in range(local_experts):
         product = jnp.dot(

time: 327 us -> 392 us (1.20)
  the two profiles are of different devices: /device:TPU:188 before, /device:TPU:56 now
where the time goes in v1:
time: 392 us; the launch traced here: 391 us
  waiting for transfers between devices  209 us (53%)
  blocking collectives  83.3 us (21%)
  starting transfers between devices  55.5 us (14%)
  matrix products  24.6 us (6%)
  local copies, waits for them, and re-layouts  9.09 us (2%)
  other arithmetic  9.01 us (2%)
    all_to_all x2, waiting for transfers between devices, body(): lax.all_to_all(results.reshape(ranks, capacity, width), 'ep', split_axis=...  130 us
    all_gather x2, blocking collectives, body(): rows = lax.all_gather(own, 'grp_1', axis=0, tiled=True)  83.3 us
    all_to_all x2, waiting for transfers between devices, body(): lax.all_to_all(jnp.stack([rows] * lax.axis_size('grp_0')), 'grp_0', 0, 0)  65.4 us
    all_to_all x2, starting transfers between devices, body(): lax.all_to_all(outgoing.reshape(ranks, capacity, hidden_width), 'ep', spl...  24.6 us
    all_to_all x2, starting transfers between devices, body(): lax.all_to_all(results.reshape(ranks, capacity, width), 'ep', split_axis=...  18.9 us
    ppermute x1, waiting for transfers between devices, body(): lax.ppermute(step_dir, 'grp_0', [(s, (s + shift) % outer) for s in range(...  13.4 us
    dot_general x2, matrix products, body(): jnp.dot(arrived[local].reshape(chunk, hidden_width), gathered[local], pre...  12.4 us
    all_to_all x2, starting transfers between devices, body(): lax.all_to_all(jnp.stack([rows] * lax.axis_size('grp_0')), 'grp_0', 0, 0)  9.29 us
  transfers between devices with their start and end apart: 7, of which 5 were waited for; matrix products, arithmetic and copies ran while one was open for 8% of the time, Pallas kernels for 0%

profile of v1, /device:TPU:56, one launch (start us, length us, event | category | flops | bytes accessed | tf_op | source)
XLA Modules:
  0.0 391.5 jit_solution(1932060789856087801)
XLA Ops:
  0.7 0.9 copy.22
  1.7 0.5 convert_reduce_fusion
  2.2 2.5 fusion.15
  4.7 15.5 %all-to-all-start = ((bf16[32,24,768]{2,1,0:T(8,128)(2,1)}), bf16[32,24,768]{2,1,0:T(8,128)(2,1)S(1)}, u32[]{:S(2)}, u32[]{:S(2)}) async-start(bf16[32,24,768]{2,1,0:T(8,128)(2,1)} %bitcast.32), calls=%async_computation | async-start | bytes 2359296 | tf_op jit(solution)/shard_map/all_to_all | solution.py:70
  20.3 2.8 subtract_convert_fusion
  23.1 0.7 fusion.60
  23.8 40.5 %all-gather = bf16[1,192,2048]{2,1,0:T(8,128)(2,1)S(1)} all-gather(bf16[1,48,2048]{2,1,0:T(8,128)(2,1)S(1)} %get-tuple-element.20), channel_id=2, replica_groups=mesh['grp_0'=4,'grp_1'=4,'ep'=32] {'grp_1'}, dimensions={1}, use_global_device_ids=true | all-gather | bytes 983040 | tf_op jit(solution)/shard_map/all_gather | solution.py:84
  64.2 2.1 stack.4
  66.3 4.6 %all-to-all-start.1 = ((bf16[4,192,2048]{2,1,0:T(8,128)(2,1)}), bf16[4,192,2048]{2,1,0:T(8,128)(2,1)}, u32[]{:S(2)}, u32[]{:S(2)}) async-start(bf16[4,192,2048]{2,1,0:T(8,128)(2,1)} %stack.4), calls=%async_computation.1 | async-start | bytes 6291456 | tf_op jit(solution)/shard_map/all_to_all | solution.py:91
  71.0 2.5 fusion.20
  73.4 34.9 %all-to-all-done.1 = bf16[4,192,2048]{2,1,0:T(8,128)(2,1)} async-done(((bf16[4,192,2048]{2,1,0:T(8,128)(2,1)}), bf16[4,192,2048]{2,1,0:T(8,128)(2,1)}, u32[]{:S(2)}, u32[]{:S(2)}) %all-to-all-start.1) | async-done | bytes 3145760 | tf_op jit(solution)/shard_map/all_to_all | solution.py:91
  108.3 9.1 %all-to-all-start.3 = ((bf16[32,24,768]{2,1,0:T(8,128)(2,1)}), bf16[32,24,768]{2,1,0:T(8,128)(2,1)}, u32[]{:S(2)}, u32[]{:S(2)}) async-start(bf16[32,24,768]{2,1,0:T(8,128)(2,1)} %bitcast.33), calls=%async_computation.3 | async-start | bytes 2359296 | tf_op jit(solution)/shard_map/all_to_all | solution.py:70
  117.4 42.8 %all_gather.7 = bf16[192,2048]{1,0:T(8,128)(2,1)S(1)} all-gather(bf16[48,2048]{1,0:T(8,128)(2,1)} %get-tuple-element.9), channel_id=1, replica_groups=mesh['grp_0'=4,'grp_1'=4,'ep'=32] {'grp_1'}, dimensions={0}, use_global_device_ids=true | all-gather | bytes 983040 | tf_op jit(solution)/shard_map/all_gather | solution.py:84
  160.2 2.1 stack.5
  162.3 4.7 %all-to-all-start.4 = ((bf16[4,192,2048]{2,1,0:T(8,128)(2,1)}), bf16[4,192,2048]{2,1,0:T(8,128)(2,1)}, u32[]{:S(2)}, u32[]{:S(2)}) async-start(bf16[4,192,2048]{2,1,0:T(8,128)(2,1)} %stack.5), calls=%async_computation.4 | async-start | bytes 6291456 | tf_op jit(solution)/shard_map/all_to_all | solution.py:91
  166.9 5.9 %multiply_convert_fusion.1 = bf16[768,2048]{1,0:T(8,128)(2,1)} fusion(bf16[768,768]{1,0:T(8,128)(2,1)S(1)} %bitcast.31, bf16[768,2048]{1,0:T(8,128)(2,1)} %bitcast.4), kind=kOutput, calls=%fused_computation.1 | convolution fusion | flops 2419064832 | bytes 7471104 | tf_op jit(solution)/shard_map/dot_general | solution.py:96
  172.8 30.5 %all-to-all-done.4 = bf16[4,192,2048]{2,1,0:T(8,128)(2,1)} async-done(((bf16[4,192,2048]{2,1,0:T(8,128)(2,1)}), bf16[4,192,2048]{2,1,0:T(8,128)(2,1)}, u32[]{:S(2)}, u32[]{:S(2)}) %all-to-all-start.4) | async-done | bytes 3145760 | tf_op jit(solution)/shard_map/all_to_all | solution.py:91
  203.3 9.6 %all-to-all-start.2 = ((bf16[32,24,2048]{2,1,0:T(8,128)(2,1)}), bf16[32,24,2048]{2,1,0:T(8,128)(2,1)}, u32[]{:S(2)}, u32[]{:S(2)}) async-start(bf16[32,24,2048]{2,1,0:T(8,128)(2,1)} %bitcast.29), calls=%async_computation.2 | async-start | bytes 6291456 | tf_op jit(solution)/shard_map/all_to_all | solution.py:104
  212.9 6.5 %multiply_convert_fusion = bf16[768,2048]{1,0:T(8,128)(2,1)} fusion(bf16[768,768]{1,0:T(8,128)(2,1)} %bitcast.9, bf16[768,2048]{1,0:T(8,128)(2,1)} %bitcast.10), kind=kOutput, calls=%fused_computation | convolution fusion | flops 2419064832 | bytes 7471104 | tf_op jit(solution)/shard_map/dot_general | solution.py:96
  219.5 74.3 %all-to-all-done.2 = bf16[32,24,2048]{2,1,0:T(8,128)(2,1)} async-done(((bf16[32,24,2048]{2,1,0:T(8,128)(2,1)}), bf16[32,24,2048]{2,1,0:T(8,128)(2,1)}, u32[]{:S(2)}, u32[]{:S(2)}) %all-to-all-start.2) | async-done | bytes 3145760 | tf_op jit(solution)/shard_map/all_to_all | solution.py:104
  293.8 9.3 %all-to-all-start.5 = ((bf16[32,24,2048]{2,1,0:T(8,128)(2,1)}), bf16[32,24,2048]{2,1,0:T(8,128)(2,1)}, u32[]{:S(2)}, u32[]{:S(2)}) async-start(bf16[32,24,2048]{2,1,0:T(8,128)(2,1)} %bitcast.28), calls=%async_computation.5 | async-start | bytes 6291456 | tf_op jit(solution)/shard_map/all_to_all | solution.py:104
  303.1 2.6 collective-permute-start
  305.9 0.7 copy.25
  306.6 0.7 copy.26
  307.4 0.8 copy.24
  308.2 4.6 %fusion.2 = (bf16[128,768]{1,0:T(8,128)(2,1)S(1)}, bf16[128,768]{1,0:T(8,128)(2,1)S(1)}, bf16[128,768]{1,0:T(8,128)(2,1)S(1)}, bf16[128,768]{1,0:T(8,128)(2,1)S(1)}) fusion(f32[128,8]{1,0:T(8,128)} %copy.26, s32[768]{0:T(1024)S(1)} %get-tuple-element.25, s32[128,8]{1,0:T(8,128)} %copy.24, s32[768]{0:T(1024)S(1)} %get-tuple-element.24, f32[128,8]{1,0:T(8,128)} %copy.25), kind=kLoop, calls=%fused_computation.10 | loop fusion | flops 7471104 | bytes 804864 | tf_op jit(solution)/shard_map/reduce_sum | solution.py:110
  312.8 13.4 %collective-permute-done = f32[2,48,2048]{2,1,0:T(8,128)S(1)} collective-permute-done((f32[2,48,2048]{2,1,0:T(8,128)S(1)}, f32[2,48,2048]{2,1,0:T(8,128)S(1)}, u32[]{:S(2)}, u32[]{:S(2)}) %collective-permute-start) | collective-permute-done | bytes 786464 | tf_op jit(solution)/shard_map/ppermute | solution.py:52
  326.1 4.2 %fusion.34 = f32[256,2048]{1,0:T(8,128)} fusion(bf16[768,2048]{1,0:T(8,128)(2,1)} %bitcast.7, bf16[128,768]{1,0:T(8,128)(2,1)S(1)} %get-tuple-element.14, bf16[128,768]{1,0:T(8,128)(2,1)S(1)} %get-tuple-element.17), kind=kOutput, calls=%fused_computation.40 | convolution fusion | flops 806092800 | bytes 5636096 | tf_op jit(solution)/shard_map/dot_general | solution.py:112
  330.4 56.2 %all-to-all-done.5 = bf16[32,24,2048]{2,1,0:T(8,128)(2,1)} async-done(((bf16[32,24,2048]{2,1,0:T(8,128)(2,1)}), bf16[32,24,2048]{2,1,0:T(8,128)(2,1)}, u32[]{:S(2)}, u32[]{:S(2)}) %all-to-all-start.5) | async-done | bytes 3145760 | tf_op jit(solution)/shard_map/all_to_all | solution.py:104
  386.5 3.0 fusion.38
  389.6 1.0 fusion.25
  390.6 0.9 copy.28
  (21 shorter events, 0.3 us)
Async XLA Ops:
  0.6 1.6 copy-start
  2.2 18.0 %copy-start.2 = (f32[2,48,2048]{2,1,0:T(8,128)S(1)}, f32[2,48,2048]{2,1,0:T(8,128)}, u32[]{:S(2)}) copy-start(f32[2,48,2048]{2,1,0:T(8,128)} %param.10) | copy-start | bytes 2359300
  4.7 59.5 %all-to-all-start = ((bf16[32,24,768]{2,1,0:T(8,128)(2,1)}), bf16[32,24,768]{2,1,0:T(8,128)(2,1)S(1)}, u32[]{:S(2)}, u32[]{:S(2)}) async-start(bf16[32,24,768]{2,1,0:T(8,128)(2,1)} %bitcast.32), calls=%async_computation | async-start | bytes 2359296 | tf_op jit(solution)/shard_map/all_to_all | solution.py:70
  66.3 42.0 %all-to-all-start.1 = ((bf16[4,192,2048]{2,1,0:T(8,128)(2,1)}), bf16[4,192,2048]{2,1,0:T(8,128)(2,1)}, u32[]{:S(2)}, u32[]{:S(2)}) async-start(bf16[4,192,2048]{2,1,0:T(8,128)(2,1)} %stack.4), calls=%async_computation.1 | async-start | bytes 6291456 | tf_op jit(solution)/shard_map/all_to_all | solution.py:91
  108.3 51.9 %all-to-all-start.3 = ((bf16[32,24,768]{2,1,0:T(8,128)(2,1)}), bf16[32,24,768]{2,1,0:T(8,128)(2,1)}, u32[]{:S(2)}, u32[]{:S(2)}) async-start(bf16[32,24,768]{2,1,0:T(8,128)(2,1)} %bitcast.33), calls=%async_computation.3 | async-start | bytes 2359296 | tf_op jit(solution)/shard_map/all_to_all | solution.py:70
  162.3 41.0 %all-to-all-start.4 = ((bf16[4,192,2048]{2,1,0:T(8,128)(2,1)}), bf16[4,192,2048]{2,1,0:T(8,128)(2,1)}, u32[]{:S(2)}, u32[]{:S(2)}) async-start(bf16[4,192,2048]{2,1,0:T(8,128)(2,1)} %stack.5), calls=%async_computation.4 | async-start | bytes 6291456 | tf_op jit(solution)/shard_map/all_to_all | solution.py:91
  203.3 90.5 %all-to-all-start.2 = ((bf16[32,24,2048]{2,1,0:T(8,128)(2,1)}), bf16[32,24,2048]{2,1,0:T(8,128)(2,1)}, u32[]{:S(2)}, u32[]{:S(2)}) async-start(bf16[32,24,2048]{2,1,0:T(8,128)(2,1)} %bitcast.29), calls=%async_computation.2 | async-start | bytes 6291456 | tf_op jit(solution)/shard_map/all_to_all | solution.py:104
  293.8 9.3 %copy-start.3 = (f32[2,48,2048]{2,1,0:T(8,128)S(1)}, f32[2,48,2048]{2,1,0:T(8,128)}, u32[]{:S(2)}) copy-start(f32[2,48,2048]{2,1,0:T(8,128)} %get-tuple-element.19) | copy-start | bytes 2359300
  293.8 12.1 %copy-start.5 = (s32[128,8]{0,1:T(8,128)S(1)}, s32[128,8]{0,1:T(8,128)}, u32[]{:S(2)}) copy-start(s32[128,8]{0,1:T(8,128)} %param.9) | copy-start | bytes 12292
  293.8 13.6 %copy-start.4 = (s32[128,8]{0,1:T(8,128)S(1)}, s32[128,8]{0,1:T(8,128)}, u32[]{:S(2)}) copy-start(s32[128,8]{0,1:T(8,128)} %param.8) | copy-start | bytes 12292
  293.8 92.7 %all-to-all-start.5 = ((bf16[32,24,2048]{2,1,0:T(8,128)(2,1)}), bf16[32,24,2048]{2,1,0:T(8,128)(2,1)}, u32[]{:S(2)}, u32[]{:S(2)}) async-start(bf16[32,24,2048]{2,1,0:T(8,128)(2,1)} %bitcast.28), calls=%async_computation.5 | async-start | bytes 6291456 | tf_op jit(solution)/shard_map/all_to_all | solution.py:104
  303.1 23.0 %collective-permute-start = (f32[2,48,2048]{2,1,0:T(8,128)S(1)}, f32[2,48,2048]{2,1,0:T(8,128)S(1)}, u32[]{:S(2)}, u32[]{:S(2)}) collective-permute-start(f32[2,48,2048]{2,1,0:T(8,128)S(1)} %copy-done.3), channel_id=1, source_target_pairs={{0,256},{128,384},{256,0},{384,128},{1,257},{129,385},{257,1},{385... | collective-permute-start | bytes 2359304 | tf_op jit(solution)/shard_map/ppermute | solution.py:52
  386.5 3.0 copy-start.1
